TPU v7x, 256 devices: a whole 4x4x8 slice. The times are simulated.
256 devices in a mesh: walker: 32 (over z, x_lo, core), vec: 8 (over x_hi, y).
Axes of the slice: x: 4 (x_hi: 2, x_lo: 2; x = x_hi * 2 + x_lo), y: 4, z: 8, core: 2. Of those that a mesh axis runs over, the one named last changes fastest.
Arguments:
- copy_counts: int32 [32], P('walker'), may hold values from 0 to 2, as said below
- panels: bfloat16 [32, 200, 2048], P('walker', 'vec'), may hold values from -6 to 6
- inverse_intersection: bfloat16 [32, 200, 200], P('walker', 'vec'), may hold values from -0.4375 to 0.4375
- trial_orbitals: bfloat16 [200, 2048], replicated, may hold values from -0.0625 to 0.0625
- chol_tiles: bfloat16 [256, 128, 128], P(('walker', 'vec')), may hold values from -1.25 to 1.25
- tile_blocks: int32 [256, 2], replicated, may hold values from 0 to 15
- aux_fields: float32 [32, 64], P('walker'), may hold values from -6 to 6
Outputs:
- new_panels: bfloat16 [32, 200, 2048], P('walker', 'vec')
Inputs may be any that keep to these rules, and one draw needn't show every extreme that they name: `copy_counts`: for k = 0 .. 32 let e_k be the sum of the counts of walkers 0 .. k - 1 minus k. Every e_k lies in 0 .. 1, the first and the last are 0 (the counts sum to 32), and e_k = 1 for at least one k. Some walker has exactly 2 copies.
All inputs are finite; a program needn't handle non-finite values.
Results may differ from a plain program's by a relative error of at most 0.007.
Values may be sent and summed in bfloat16 or wider, within the bound.
No kernel may reach another device: no remote copies, remote signals or barrier semaphores. Data moves between devices by JAX's collectives and lax.ppermute only.
A program may use at most 64 MiB of HBM per device.

v0:
```python
import math
import jax
import jax.numpy as jnp
from jax import lax
from jax.sharding import PartitionSpec as P

KT = 4
TERMS = 3
TIME_STEP_ROOT = 0.1


def from_behind(value, axis, steps):
    count = lax.axis_size(axis)
    leading, last = (max(0, -steps), min(count, count - steps))
    return lax.ppermute(value, axis, [(source, source + steps) for source in range(leading, last)])


def tile_bias(tile_piece, row_blocks, col_blocks, panel_blocks, green_blocks):
    chosen = jnp.take(green_blocks, col_blocks, axis=2)
    product = jnp.einsum("wirl,rkl->wirk", chosen, tile_piece, preferred_element_type=jnp.float32)
    facing = jnp.take(panel_blocks, row_blocks, axis=2)
    return jnp.sum(product * facing, axis=(1, 3))


def force_bias(walker_panels, walker_inverse, trial_orbitals, chol_tiles, tile_blocks):
    walkers, cols_local, orbitals = walker_panels.shape
    tile_size = chol_tiles.shape[1]
    block_count = orbitals // tile_size
    tiles_total = tile_blocks.shape[0]
    green_rows = jnp.einsum(
        "wij,jm->wim", walker_inverse, trial_orbitals, preferred_element_type=jnp.float32
    ).astype(jnp.bfloat16)
    panel_blocks = walker_panels.reshape(walkers, cols_local, block_count, tile_size)
    green_blocks = green_rows.reshape(walkers, cols_local, block_count, tile_size)
    tile_piece = lax.all_gather(chol_tiles, ("walker", "vec"), axis=0, tiled=True)
    contrib = tile_bias(
        tile_piece, tile_blocks[:, 0], tile_blocks[:, 1], panel_blocks, green_blocks
    )
    partial_bias = contrib
    stored = tile_piece
    partial_bias, stored = (partial_bias, stored)
    per_vector = partial_bias.reshape(walkers, tiles_total // KT, KT).sum(axis=2)
    summed_bias = lax.psum(per_vector, "vec")
    return (jnp.clip(TIME_STEP_ROOT * summed_bias, -1.0, 1.0), stored)


def propagate(start_panels, scales, stored, tile_blocks):
    slot_count, cols_local, orbitals = start_panels.shape
    tile_size = stored.shape[1]
    block_count = orbitals // tile_size
    tiles_total = stored.shape[0]
    step_tiles = math.gcd(tiles_total, 256)
    rows_hot = (
        tile_blocks[:, 0][None, :] == jnp.arange(block_count, dtype=jnp.int32)[:, None]
    ).astype(jnp.float32)
    weights = jnp.repeat(scales, KT, axis=1)[:, None, :] * rows_hot[None, :, :]
    col_blocks = tile_blocks[:, 1]
    running = start_panels.astype(jnp.float32)
    series = start_panels
    for degree in range(1, TERMS + 1):
        series_blocks = series.reshape(slot_count, cols_local, block_count, tile_size)

        def add_block(block_index, summed):
            chosen = jnp.take(series_blocks, col_blocks, axis=2)
            product = jnp.einsum(
                "qitl,tkl->qitk", chosen, stored, preferred_element_type=jnp.float32
            )
            return summed + jnp.einsum(
                "qitk,qat->qiak", product, weights, precision=lax.Precision.HIGHEST
            )

        result = lax.fori_loop(
            0,
            tiles_total // step_tiles,
            add_block,
            jnp.zeros((slot_count, cols_local, block_count, tile_size), jnp.float32),
        )
        series = (result / degree).reshape(slot_count, cols_local, orbitals).astype(jnp.bfloat16)
        running = running + series.astype(jnp.float32)
    return running.astype(jnp.bfloat16)


def shards(
    copy_counts, panels, inverse_intersection, trial_orbitals, chol_tiles, tile_blocks, aux_fields
):
    walkers = panels.shape[0]
    every_count = lax.all_gather(copy_counts, "walker", axis=0, tiled=True)
    running_sum = jnp.cumsum(every_count)
    first_slot = lax.axis_index("walker") * walkers
    bias, stored = force_bias(panels, inverse_intersection, trial_orbitals, chol_tiles, tile_blocks)
    own_sums = lax.dynamic_slice_in_dim(running_sum, first_slot, walkers, 0)
    surplus = own_sums[0] - copy_counts[0] - first_slot
    new_index = first_slot + jnp.arange(2 * walkers, dtype=jnp.int32)
    parent = jnp.minimum(
        jnp.sum((own_sums[None, :] <= new_index[:, None]).astype(jnp.int32), axis=1), walkers - 1
    )
    right_fields = from_behind(aux_fields, "walker", -1)
    field_pool = jnp.concatenate([aux_fields, right_fields], axis=0)
    scales = TIME_STEP_ROOT * (field_pool - jnp.take(bias, parent, axis=0))
    copies = propagate(jnp.take(panels, parent, axis=0), scales, stored, tile_blocks)
    arrived = from_behind(copies[walkers:], "walker", 1)
    keep_own = (jnp.arange(walkers, dtype=jnp.int32) >= surplus)[:, None, None]
    return jnp.where(keep_own, copies[:walkers], arrived)


def solution(mesh):
    return jax.shard_map(
        shards,
        mesh=mesh,
        in_specs=(
            P("walker"),
            P("walker", "vec", None),
            P("walker", "vec", None),
            P(),
            P(("walker", "vec"), None, None),
            P(),
            P("walker", None),
        ),
        out_specs=P("walker", "vec", None),
        check_vma=False,
    )
```

profile of v0, /device:TPU:104, one launch (start us, length us, event | category | flops | bytes accessed | tf_op | source)
XLA Modules:
  0.0 873.2 jit_solution(1294676800339931212)
XLA Ops:
  6.5 0.7 all-gather.2.cloned.1.call-update
  7.3 2.4 collective-permute-start
  9.7 1.0 convolution_convert_fusion
  10.8 0.9 copy.50
  12.4 1.2 dynamic-slice.1
  13.6 0.7 dynamic-update-slice
  14.3 16.2 %all-reduce = s32[32]{0:T(128)S(1)} all-reduce(s32[32]{0:T(128)S(1)} %dynamic-update-slice), channel_id=1, replica_groups=mesh['walker'=32,'vec'=8] {'walker'}, use_global_device_ids=true, to_apply=%add | all-reduce | flops 32 | bytes 256
  30.7 0.8 fusion.82
  31.4 1.0 gather_fusion
  33.0 0.6 compare_and_fusion.2
  33.9 15.0 %gather_fusion.2 = bf16[256,2,25,128]{3,1,2,0:T(2,128)(2,1)} fusion(bf16[2,25,16,128]{3,0,2,1:T(2,128)(2,1)S(1)} %broadcast_select_fusion.3, s32[1024]{0:T(1024)S(1)} %pad_clamp_fusion.1), kind=kCustom, calls=%fused_computation.1.clone | custom fusion | bytes 6554624 | tf_op jit(solution)/shard_map/while/body/eval_jaxpr/jit(_take)/gather | solution.py:64
  48.9 2.3 gather_fusion.1
  51.2 6.8 fusion.16
  58.0 653.9 %all-gather.2.cloned.1.call-done = bf16[256,128,128]{2,1,0:T(8,128)(2,1)} async-done(((bf16[1,128,128]{2,1,0:T(8,128)(2,1)}), bf16[256,128,128]{2,1,0:T(8,128)(2,1)}) %all-gather.2.cloned.1.call-update) | async-done | bytes 8388624 | tf_op jit(solution)/shard_map/all_gather | solution.py:35
  711.9 8.1 fusion.12
  720.2 45.2 %psum.7 = f32[1,64]{1,0:T(1,128)S(1)} all-reduce(f32[1,64]{1,0:T(1,128)S(1)} %bitcast.126), channel_id=1, replica_groups=mesh['walker'=32,'vec'=8] {'vec'}, use_global_device_ids=true, to_apply=%region_3.5 | all-reduce | flops 64 | bytes 512 | tf_op jit(solution)/shard_map/psum | solution.py:43
  765.7 10.2 %fusion.19 = f32[2,25,256,128]{3,1,0,2:T(8,128)S(1)} fusion(bf16[256,128,128]{2,1,0:T(8,128)(2,1)} %all-gather.2.cloned.1.call-done, bf16[2,25,256,128]{3,0,1,2:T(2,128)(2,1)} %fusion.16), kind=kOutput, calls=%fused_computation.28 | convolution fusion | flops 419430400 | bytes 18219008 | tf_op jit(solution)/shard_map/while/body/eval_jaxpr/qitl,tkl->qitk/dot_general | solution.py:65
  775.9 6.8 fusion.58
  782.8 15.4 %gather_fusion.3 = bf16[256,2,25,128]{3,1,2,0:T(2,128)(2,1)} fusion(bf16[2,25,16,128]{3,0,2,1:T(2,128)(2,1)S(1)} %copy.38, s32[1024]{0:T(1024)S(1)} %pad_clamp_fusion.1), kind=kCustom, calls=%fused_computation.3.clone | custom fusion | bytes 6554624 | tf_op jit(solution)/shard_map/while/body/eval_jaxpr/jit(_take)/gather | solution.py:64
  798.2 5.0 fusion.17
  803.3 8.3 fusion.24
  811.6 6.8 fusion.61
  818.5 0.8 copy.41
  819.3 0.8 copy.37
  820.1 15.2 %gather_fusion.4 = bf16[256,2,25,128]{3,1,2,0:T(2,128)(2,1)} fusion(bf16[2,25,16,128]{3,0,2,1:T(2,128)(2,1)S(1)} %copy.42, s32[1024]{0:T(1024)S(1)} %pad_clamp_fusion.1), kind=kCustom, calls=%fused_computation.4.clone | custom fusion | bytes 6554624 | tf_op jit(solution)/shard_map/while/body/eval_jaxpr/jit(_take)/gather | solution.py:64
  835.2 5.0 fusion.18
  840.3 8.4 fusion.29
  848.7 6.8 fusion.49
  856.2 0.6 add_convert_fusion
  857.0 1.9 collective-permute-start.1
  859.5 5.4 collective-permute-done.1
  865.2 0.7 copy.46
  (42 shorter events, 3.1 us)
Async XLA Ops:
  6.5 3.1 copy-start
  6.5 27.1 %copy-start.3 = (bf16[1,25,2048]{2,1,0:T(8,128)(2,1)S(1)}, bf16[1,25,2048]{2,1,0:T(8,128)(2,1)}, u32[]{:S(2)}) copy-start(bf16[1,25,2048]{2,1,0:T(8,128)(2,1)} %param.12) | copy-start | bytes 307204
  6.5 705.3 %all-gather.2.cloned.1.call-start = ((), (), s32[]{:S(2)}) async-start(), calls=%async_computation | async-start | bytes 8421376 | tf_op jit(solution)/shard_map/all_gather | solution.py:35
  7.3 758.2 %collective-permute-start = (f32[1,64]{1,0:T(1,128)}, f32[1,64]{1,0:T(1,128)S(1)}, u32[]{:S(2)}, u32[]{:S(2)}) collective-permute-start(f32[1,64]{1,0:T(1,128)} %param.17), channel_id=1, source_target_pairs={{8,0},{16,8},{24,16},{32,24},{40,32},{48,40},{56,48},{64,56},{72,6... | collective-permute-start | bytes 776 | tf_op jit(solution)/shard_map/ppermute | solution.py:15
  711.9 53.6 %copy-start.4 = (f32[1,64]{1,0:T(1,128)S(1)}, f32[1,64]{1,0:T(1,128)}, u32[]{:S(2)}) copy-start(f32[1,64]{1,0:T(1,128)} %param.17) | copy-start | bytes 772
  848.7 7.0 copy-start.1
  848.7 7.3 copy-start.2
  857.0 8.0 collective-permute-start.1
Sparse Core Ops, SparseCore 0:
  9.2 702.6 all-gather.1
where the time goes:
time: 882 us; the launch traced here: 873 us
  waiting for transfers between devices  660 us (75%)
  blocking collectives  61.4 us (7%)
  local copies, waits for them, and re-layouts  57 us (6%)
  matrix products  56.3 us (6%)
  other arithmetic  18.9 us (2%)
  between operations  15.4 us (2%)
    all_gather x1, waiting for transfers between devices, force_bias(): lax.all_gather(chol_tiles, ('walker', 'vec'), axis=0, tiled=True)  654 us
    gather x3, local copies, waits for them, and re-layouts, add_block(): chosen = jnp.take(series_blocks, col_blocks, axis=2)  45.5 us
    psum x1, blocking collectives, force_bias(): summed_bias = lax.psum(per_vector, 'vec')  45.2 us
    dot_general x3, matrix products, add_block(): jnp.einsum('qitl,tkl->qitk', chosen, stored, preferred_element_type=jnp.f...  26.9 us
    dot_general x3, matrix products, add_block(): jnp.einsum('qitk,qat->qiak', product, weights, precision=lax.Precision.HI...  20.3 us
  transfers between devices with their start and end apart: 3, of which 2 were waited for; matrix products, arithmetic and copies ran while one was open for 5% of the time, Pallas kernels for 0%

commit v1 on v0

--- a/solution.py
+++ b/solution.py
@@ -32,7 +32,8 @@
     ).astype(jnp.bfloat16)
     panel_blocks = walker_panels.reshape(walkers, cols_local, block_count, tile_size)
     green_blocks = green_rows.reshape(walkers, cols_local, block_count, tile_size)
-    tile_piece = lax.all_gather(chol_tiles, ("walker", "vec"), axis=0, tiled=True)
+    sent = jnp.stack([chol_tiles] * lax.axis_size(("walker", "vec")))
+    tile_piece = jnp.concatenate(lax.all_to_all(sent, ("walker", "vec"), 0, 0), axis=0)
     contrib = tile_bias(
         tile_piece, tile_blocks[:, 0], tile_blocks[:, 1], panel_blocks, green_blocks
     )

time: 882 us -> 382 us (0.43)
  the two profiles are of different devices: /device:TPU:104 before, /device:TPU:32 now
where the time goes in v1:
time: 382 us; the launch traced here: 379 us
  blocking collectives  208 us (54%)
  matrix products  64.5 us (17%)
  local copies, waits for them, and re-layouts  59.9 us (16%)
  starting transfers between devices  20.3 us (5%)
  other arithmetic  18.8 us (5%)
  waiting for transfers between devices  5.36 us (1%)
    unnamed x1, blocking collectives  183 us
    gather x3, local copies, waits for them, and re-layouts, add_block(): chosen = jnp.take(series_blocks, col_blocks, axis=2)  45.3 us
    dot_general x3, matrix products, add_block(): jnp.einsum('qitl,tkl->qitk', chosen, stored, preferred_element_type=jnp.f...  27.1 us
    psum x1, blocking collectives, force_bias(): summed_bias = lax.psum(per_vector, 'vec')  24.9 us
    dot_general x3, matrix products, add_block(): jnp.einsum('qitk,qat->qiak', product, weights, precision=lax.Precision.HI...  20.3 us
    dot_general x1, matrix products, tile_bias(): jnp.einsum('wirl,rkl->wirk', chosen, tile_piece, preferred_element_type=j...  16.9 us
    select_n x3, other arithmetic, add_block(): chosen = jnp.take(series_blocks, col_blocks, axis=2)  16.8 us
    all_to_all x1, starting transfers between devices, force_bias(): lax.all_to_all(sent, ('walker', 'vec'), 0, 0)  15.4 us
  transfers between devices with their start and end apart: 3, of which 1 were waited for; matrix products, arithmetic and copies ran while one was open for 12% of the time, Pallas kernels for 0%

profile of v1, /device:TPU:32, one launch (start us, length us, event | category | flops | bytes accessed | tf_op | source)
XLA Modules:
  0.0 379.1 jit_solution(12549227429919406584)
XLA Ops:
  0.0 6.2 %stack.2 = bf16[256,1,128,128]{3,2,1,0:T(8,128)(2,1)} broadcast(bf16[128,128]{1,0:T(8,128)(2,1)} %bitcast.126), dimensions={2,3} | broadcast | bytes 8421376 | tf_op jit(solution)/shard_map/stack | solution.py:35
  6.2 15.4 %all-to-all-start = ((bf16[256,1,128,128]{3,2,1,0:T(8,128)(2,1)}), bf16[256,1,128,128]{3,2,1,0:T(8,128)(2,1)}, u32[]{:S(2)}, u32[]{:S(2)}) async-start(bf16[256,1,128,128]{3,2,1,0:T(8,128)(2,1)} %stack.2), calls=%async_computation | async-start | bytes 16777216 | tf_op jit(solution)/shard_map/all_to_all | solution.py:36
  21.6 3.0 collective-permute-start
  24.6 0.3 convolution_convert_fusion
  25.7 0.6 dynamic-slice.1
  26.3 0.7 dynamic-update-slice
  27.0 183.5 %all-reduce = s32[32]{0:T(128)S(1)} all-reduce(s32[32]{0:T(128)S(1)} %dynamic-update-slice), channel_id=1, replica_groups=mesh['walker'=32,'vec'=8] {'walker'}, use_global_device_ids=true, to_apply=%add | all-reduce | flops 32 | bytes 256
  210.6 1.0 gather_fusion
  211.6 0.6 constant_dynamic-slice_fusion
  212.2 0.7 compare_and_fusion.2
  212.9 0.2 broadcast_select_fusion.3
  213.2 15.0 %gather_fusion.2 = bf16[256,2,25,128]{3,1,2,0:T(2,128)(2,1)} fusion(bf16[2,25,16,128]{3,0,2,1:T(2,128)(2,1)S(1)} %broadcast_select_fusion.3, s32[1024]{0:T(1024)S(1)} %pad_clamp_fusion.1), kind=kCustom, calls=%fused_computation.1.clone | custom fusion | bytes 6554624 | tf_op jit(solution)/shard_map/while/body/eval_jaxpr/jit(_take)/gather | solution.py:65
  228.2 2.2 gather_fusion.1
  230.4 6.7 %fusion.18 = bf16[2,25,256,128]{3,0,1,2:T(2,128)(2,1)} fusion(bf16[256,2,25,128]{3,1,2,0:T(2,128)(2,1)} %gather_fusion.2, pred[256]{0:T(512)(128)(4,1)S(1)} %get-tuple-element.50), kind=kLoop, calls=%fused_computation.27 | loop fusion | flops 1638400 | bytes 6553856 | tf_op jit(solution)/shard_map/while/body/eval_jaxpr/jit(_take)/select_n | solution.py:65
  237.1 16.9 %fusion.14 = f32[256]{0:T(256)S(1)} fusion(bf16[256,1,128,128]{3,2,1,0:T(8,128)(2,1)} %all-to-all-done, bf16[256,25,128]{2,1,0:T(8,128)(2,1)} %gather_fusion.1, bf16[256,25,128]{2,1,0:T(8,128)(2,1)S(1)} %gather_fusion, pred[256]{0:T(512)(128)(4,1)S(1)} %get-tuple-element.49, pred[256]{0:T(512)(128)(4,1)S(1)} %get-tuple-element.50), kind=kOutput, calls=%fused_computation.23 | convolution fusion | flops 213810944 | bytes 11666944 | tf_op jit(solution)/shard_map/wirl,rkl->wirk/dot_general | solution.py:20
  254.2 24.9 %psum.7 = f32[1,64]{1,0:T(1,128)S(1)} all-reduce(f32[1,64]{1,0:T(1,128)S(1)} %bitcast.132), channel_id=1, replica_groups=mesh['walker'=32,'vec'=8] {'vec'}, use_global_device_ids=true, to_apply=%region_3.5 | all-reduce | flops 64 | bytes 512 | tf_op jit(solution)/shard_map/psum | solution.py:44
  279.4 10.2 %fusion.21 = f32[2,25,256,128]{3,1,0,2:T(8,128)S(1)} fusion(bf16[256,1,128,128]{3,2,1,0:T(8,128)(2,1)} %all-to-all-done, bf16[2,25,256,128]{3,0,1,2:T(2,128)(2,1)} %fusion.18), kind=kOutput, calls=%fused_computation.30 | convolution fusion | flops 419430400 | bytes 18219008 | tf_op jit(solution)/shard_map/while/body/eval_jaxpr/qitl,tkl->qitk/dot_general | solution.py:66
  289.6 6.8 %fusion.62 = bf16[2,25,16,128]{3,2,1,0:T(8,128)(2,1)S(1)} fusion(f32[2,25,256,128]{3,1,0,2:T(8,128)S(1)} %fusion.21, f32[16,256]{1,0:T(8,128)S(1)} %fusion.82, f32[2,256]{1,0:T(2,128)S(1)} %mul.35), kind=kOutput, calls=%fused_computation.45 | convolution fusion | flops 314683392 | bytes 6776832 | tf_op jit(solution)/shard_map/while/body/eval_jaxpr/qitk,qat->qiak/dot_general | solution.py:69
  296.5 15.2 %gather_fusion.3 = bf16[256,2,25,128]{3,1,2,0:T(2,128)(2,1)} fusion(bf16[2,25,16,128]{3,0,2,1:T(2,128)(2,1)S(1)} %copy.38, s32[1024]{0:T(1024)S(1)} %pad_clamp_fusion.1), kind=kCustom, calls=%fused_computation.3.clone | custom fusion | bytes 6554624 | tf_op jit(solution)/shard_map/while/body/eval_jaxpr/jit(_take)/gather | solution.py:65
  311.7 5.0 %fusion.19 = bf16[2,25,256,128]{3,0,1,2:T(2,128)(2,1)S(1)} fusion(bf16[256,2,25,128]{3,1,2,0:T(2,128)(2,1)} %gather_fusion.3, pred[256]{0:T(512)(128)(4,1)S(1)} %get-tuple-element.50), kind=kLoop, calls=%fused_computation.28 | loop fusion | flops 1638400 | bytes 6553856 | tf_op jit(solution)/shard_map/while/body/eval_jaxpr/jit(_take)/select_n | solution.py:65
  316.8 8.5 %fusion.26 = f32[2,25,256,128]{3,1,0,2:T(8,128)S(1)} fusion(bf16[256,1,128,128]{3,2,1,0:T(8,128)(2,1)} %all-to-all-done, bf16[2,25,256,128]{3,0,1,2:T(2,128)(2,1)S(1)} %fusion.19), kind=kOutput, calls=%fused_computation.31 | convolution fusion | flops 419430400 | bytes 18219008 | tf_op jit(solution)/shard_map/while/body/eval_jaxpr/qitl,tkl->qitk/dot_general | solution.py:66
  325.3 6.8 %fusion.65 = bf16[2,25,16,128]{3,2,1,0:T(8,128)(2,1)S(1)} fusion(f32[2,25,256,128]{3,1,0,2:T(8,128)S(1)} %fusion.26, f32[16,256]{1,0:T(8,128)S(1)} %fusion.82, f32[2,256]{1,0:T(2,128)S(1)} %mul.35), kind=kOutput, calls=%fused_computation.46 | convolution fusion | flops 314785792 | bytes 6776832 | tf_op jit(solution)/shard_map/while/body/eval_jaxpr/qitk,qat->qiak/dot_general | solution.py:69
  332.3 0.8 copy.37
  333.1 15.1 %gather_fusion.4 = bf16[256,2,25,128]{3,1,2,0:T(2,128)(2,1)} fusion(bf16[2,25,16,128]{3,0,2,1:T(2,128)(2,1)S(1)} %copy.42, s32[1024]{0:T(1024)S(1)} %pad_clamp_fusion.1), kind=kCustom, calls=%fused_computation.4.clone | custom fusion | bytes 6554624 | tf_op jit(solution)/shard_map/while/body/eval_jaxpr/jit(_take)/gather | solution.py:65
  348.2 5.0 %fusion.20 = bf16[2,25,256,128]{3,0,1,2:T(2,128)(2,1)S(1)} fusion(bf16[256,2,25,128]{3,1,2,0:T(2,128)(2,1)} %gather_fusion.4, pred[256]{0:T(512)(128)(4,1)S(1)} %get-tuple-element.50), kind=kLoop, calls=%fused_computation.29 | loop fusion | flops 1638400 | bytes 6553856 | tf_op jit(solution)/shard_map/while/body/eval_jaxpr/jit(_take)/select_n | solution.py:65
  353.2 8.3 %fusion.31 = f32[2,25,256,128]{3,1,0,2:T(8,128)S(1)} fusion(bf16[256,1,128,128]{3,2,1,0:T(8,128)(2,1)} %all-to-all-done, bf16[2,25,256,128]{3,0,1,2:T(2,128)(2,1)S(1)} %fusion.20), kind=kOutput, calls=%fused_computation.32 | convolution fusion | flops 419430400 | bytes 18219008 | tf_op jit(solution)/shard_map/while/body/eval_jaxpr/qitl,tkl->qitk/dot_general | solution.py:66
  361.6 6.8 %fusion.53 = f32[2,25,16,128]{3,2,1,0:T(8,128)S(1)} fusion(f32[2,25,256,128]{3,1,0,2:T(8,128)S(1)} %fusion.31, f32[16,256]{1,0:T(8,128)S(1)} %fusion.82, f32[2,256]{1,0:T(2,128)S(1)} %mul.35), kind=kOutput, calls=%fused_computation.42 | convolution fusion | flops 314888192 | bytes 6981632 | tf_op jit(solution)/shard_map/while/body/eval_jaxpr/qitk,qat->qiak/dot_general | solution.py:69
  369.1 0.5 add_convert_fusion
  369.9 1.9 collective-permute-start.1
  372.5 5.4 %collective-permute-done.1 = bf16[1,25,2048]{2,0,1:T(2,128)(2,1)S(1)} collective-permute-done((bf16[1,25,2048]{2,0,1:T(2,128)(2,1)S(1)}, bf16[1,25,2048]{2,0,1:T(2,128)(2,1)S(1)}, u32[]{:S(2)}, u32[]{:S(2)}) %collective-permute-start.1) | collective-permute-done | bytes 102432 | tf_op jit(solution)/shard_map/ppermute | solution.py:15
  377.8 0.3 broadcast_select_fusion.4
  378.1 0.7 copy.46
  (48 shorter events, 2.1 us)
Async XLA Ops:
  0.0 24.6 %copy-start = (bf16[200,2048]{1,0:T(8,128)(2,1)S(1)}, bf16[200,2048]{1,0:T(8,128)(2,1)}, u32[]{:S(2)}) copy-start(bf16[200,2048]{1,0:T(8,128)(2,1)} %param.14) | copy-start | bytes 2457604
  6.2 15.4 %copy-start.6 = (f32[1,64]{1,0:T(1,128)S(1)}, f32[1,64]{1,0:T(1,128)}, u32[]{:S(2)}) copy-start(f32[1,64]{1,0:T(1,128)} %param.17) | copy-start | bytes 772
  6.2 18.4 %copy-start.4 = (bf16[1,25,200]{2,1,0:T(8,128)(2,1)S(1)}, bf16[1,25,200]{2,1,0:T(8,128)(2,1)}, u32[]{:S(2)}) copy-start(bf16[1,25,200]{2,1,0:T(8,128)(2,1)} %param.13) | copy-start | bytes 30004
  6.2 18.8 %copy-start.3 = (bf16[1,25,2048]{2,1,0:T(8,128)(2,1)S(1)}, bf16[1,25,2048]{2,1,0:T(8,128)(2,1)}, u32[]{:S(2)}) copy-start(bf16[1,25,2048]{2,1,0:T(8,128)(2,1)} %param.12) | copy-start | bytes 307204
  6.2 19.5 %copy-start.7 = (u32[256]{0:T(256)S(1)}, u32[256]{0:T(256)}, u32[]{:S(2)}) copy-start(u32[256]{0:T(256)} %constant.93) | copy-start | bytes 3076
  6.2 204.4 %copy-start.5 = (s32[256,2]{0,1:T(2,128)S(1)}, s32[256,2]{0,1:T(2,128)}, u32[]{:S(2)}) copy-start(s32[256,2]{0,1:T(2,128)} %param.16) | copy-start | bytes 6148
  6.2 230.9 %all-to-all-start = ((bf16[256,1,128,128]{3,2,1,0:T(8,128)(2,1)}), bf16[256,1,128,128]{3,2,1,0:T(8,128)(2,1)}, u32[]{:S(2)}, u32[]{:S(2)}) async-start(bf16[256,1,128,128]{3,2,1,0:T(8,128)(2,1)} %stack.2), calls=%async_computation | async-start | bytes 16777216 | tf_op jit(solution)/shard_map/all_to_all | solution.py:36
  21.6 257.5 %collective-permute-start = (f32[1,64]{1,0:T(1,128)S(1)}, f32[1,64]{1,0:T(1,128)S(1)}, u32[]{:S(2)}, u32[]{:S(2)}) collective-permute-start(f32[1,64]{1,0:T(1,128)S(1)} %copy-done.6), channel_id=1, source_target_pairs={{8,0},{16,8},{24,16},{32,24},{40,32},{48,40},{56,48},{64,56},{72,6... | collective-permute-start | bytes 776 | tf_op jit(solution)/shard_map/ppermute | solution.py:15
  361.6 7.3 %copy-start.2 = (f32[2,25,16,128]{3,2,0,1:T(8,128)S(1)}, f32[2,25,16,128]{3,2,0,1:T(8,128)}, u32[]{:S(2)}) copy-start(f32[2,25,16,128]{3,2,0,1:T(8,128)} %copy.37) | copy-start | bytes 1228804
  361.6 17.3 %copy-start.1 = (bf16[200,2048]{1,0:T(8,128)(2,1)S(1)}, bf16[200,2048]{1,0:T(8,128)(2,1)}, u32[]{:S(2)}) copy-start(bf16[200,2048]{1,0:T(8,128)(2,1)} %param.14) | copy-start | bytes 2457604
  369.9 8.0 %collective-permute-start.1 = (bf16[1,25,2048]{2,0,1:T(2,128)(2,1)S(1)}, bf16[1,25,2048]{2,0,1:T(2,128)(2,1)S(1)}, u32[]{:S(2)}, u32[]{:S(2)}) collective-permute-start(bf16[1,25,2048]{2,0,1:T(2,128)(2,1)S(1)} %slice.29), channel_id=1, source_target_pairs={{0,8},{8,16},{16,24},{24,32},{32,40},{40,48},{48,56},{56,64},{64,7... | collective-permute-start | bytes 307208 | tf_op jit(solution)/shard_map/ppermute | solution.py:15
